TPU v7x, 128 devices: a whole 4x4x4 slice. The times are simulated.
128 devices in a mesh: dp: 8 (over x, core), pair: 16 (over z, y).
Axes of the slice: x: 4, y: 4, z: 4, core: 2. Of those that a mesh axis runs over, the one named last changes fastest.
Arguments:
- anchor: bfloat16 [5, 4096, 1024], P(None, ('dp', 'pair')), may hold values from -20 to 20
- partner: bfloat16 [5, 4096, 1024], P(None, ('dp', 'pair')), may hold values from -12 to 12
- counts: int32 [5], replicated, may hold values from 512 to 4096, as said below
- pair_scale: float32 [5], replicated, may hold values from 2 to 8
Outputs:
- loss_value: float32 [], replicated
- grad_anchor: float32 [5, 4096, 1024], P(None, ('dp', 'pair'))
- grad_partner: float32 [5, 4096, 1024], P(None, ('dp', 'pair'))
Inputs may be any that keep to these rules, and one draw needn't show every extreme that they name: The valid samples of pair p are its rows 0 to counts[p] - 1; one pair has all 4096 rows valid.
All inputs are finite; a program needn't handle non-finite values.
Results may differ from a plain program's by a relative error of at most 0.0021.
Values may be sent and summed in bfloat16 or wider, within the bound.
No kernel may reach another device: no remote copies, remote signals or barrier semaphores. Data moves between devices by JAX's collectives and lax.ppermute only.
A program may use at most 128 MiB of HBM per device.

v0:
```python
import math
import jax
import jax.numpy as jnp
from jax import lax
from jax.sharding import PartitionSpec as P

NEG = -1e30


def merge_pair(mine, other):
    highest = jnp.maximum(mine[0], other[0])
    summed = mine[1] * jnp.exp(mine[0] - highest) + other[1] * jnp.exp(other[0] - highest)
    return jnp.concatenate([highest[None], summed[None], mine[2:] + other[2:]], axis=0)


def butterfly_merge(stats, axis, size):
    own = lax.axis_index(axis)
    bit = 1
    while bit < size:
        other = lax.ppermute(stats, axis, [(i, i ^ bit) for i in range(size)])
        lower = own & bit == 0
        stats = merge_pair(jnp.where(lower, stats, other), jnp.where(lower, other, stats))
        bit *= 2
    return stats


def group_merge(stats, axis, stride, group):
    own = lax.axis_index(axis)
    digit = own // stride % group
    size = lax.axis_size(axis)
    received = [stats]
    for shift in range(1, group):
        perm = [
            (i, i + ((i // stride + shift) % group - i // stride % group) * stride)
            for i in range(size)
        ]
        received.append(lax.ppermute(stats, axis, perm))
    stacked = jnp.stack(received)
    ordered = jnp.take(stacked, (digit - jnp.arange(group)) % group, axis=0)
    merged = ordered[0]
    for member in range(1, group):
        merged = merge_pair(merged, ordered[member])
    return merged


def butterfly_sum(values, axis, size):
    own = lax.axis_index(axis)
    bit = 1
    while bit < size:
        other = lax.ppermute(values, axis, [(i, i ^ bit) for i in range(size)])
        lower = own & bit == 0
        values = jnp.where(lower, values, other) + jnp.where(lower, other, values)
        bit *= 2
    return values


def ring_position(offset, size):
    return (offset + size // 2) % size


def ring_gather(shard, axis, size):
    forward = [(i, (i + 1) % size) for i in range(size)]
    backward = [(i, (i - 1) % size) for i in range(size)]
    parts = [None] * size
    parts[ring_position(0, size)] = shard
    ahead = shard
    behind = shard
    forward_steps = size // 2
    backward_steps = size - 1 - forward_steps
    for step in range(1, forward_steps + 1):
        ahead = lax.ppermute(ahead, axis, forward)
        parts[ring_position(-step, size)] = ahead
        if step <= backward_steps:
            behind = lax.ppermute(behind, axis, backward)
            parts[ring_position(step, size)] = behind
    return parts


def two_stage_reduce_scatter(grad_cols, extra, axis, size, shard_rows):
    pair_count, _, width = grad_cols.shape
    own = lax.axis_index(axis)
    parity = own % 2
    chips = size // 2
    by_chip = grad_cols.reshape(pair_count, chips, 2, shard_rows, width)
    keep = lax.dynamic_index_in_dim(by_chip, parity, axis=2, keepdims=False)
    send = lax.dynamic_index_in_dim(by_chip, 1 - parity, axis=2, keepdims=False)
    body_rows = pair_count * chips * shard_rows
    send = jnp.concatenate([send.reshape(body_rows, width), extra], axis=0)
    got = lax.ppermute(send, axis, [(i, i ^ 1) for i in range(size)])
    summed = keep + got[:body_rows].reshape(pair_count, chips, shard_rows, width)
    carried = extra + got[body_rows:]
    chip = own // 2
    ring = [(i, (i + 2) % size) for i in range(size)]
    chunk_rows = pair_count * shard_rows

    def addend(target):
        block = lax.dynamic_index_in_dim(summed, target % chips, axis=1, keepdims=False)
        return jnp.concatenate([block.reshape(chunk_rows, width), carried], axis=0)

    running = addend(chip - 1)
    for step in range(1, chips):
        running = lax.ppermute(running, axis, ring) + addend(chip - 1 - step)
    return (running[:chunk_rows].reshape(pair_count, shard_rows, width), running[chunk_rows])


def per_device(anchor, partner, counts, pair_scale):
    pair_count, shard_rows, model_width = anchor.shape
    score_scale = 4.0 / math.sqrt(model_width)
    dp_size = lax.axis_size("dp")
    pair_size = lax.axis_size("pair")
    dp_index = lax.axis_index("dp")
    pair_place = lax.axis_index("pair")
    own_first = (dp_index * pair_size + pair_place) * shard_rows
    offsets = jnp.arange(shard_rows, dtype=jnp.int32)
    own_valid = own_first + offsets[None, :] < counts[:, None]
    positive = (
        jnp.sum(anchor.astype(jnp.float32) * partner.astype(jnp.float32), axis=2) * score_scale
    )
    own_positive = jnp.sum(jnp.where(own_valid, positive, 0.0), axis=1)
    row_set = lax.all_gather(anchor, "pair", axis=1, tiled=True)
    col_set = jnp.concatenate(ring_gather(partner, "dp", dp_size), axis=1)
    col_set = jnp.roll(col_set, (dp_index - dp_size // 2) * shard_rows, axis=1)
    row_count = row_set.shape[1]
    col_count = col_set.shape[1]
    row_global = dp_index * row_count + jnp.arange(row_count, dtype=jnp.int32)
    col_first = (jnp.arange(dp_size, dtype=jnp.int32) * pair_size + pair_place) * shard_rows
    col_global = (col_first[:, None] + offsets[None, :]).reshape(-1)
    row_valid = row_global[None, :] < counts[:, None]
    col_valid = col_global[None, :] < counts[:, None]
    inside = row_valid[:, :, None] & col_valid[:, None, :]
    scores = (
        jnp.einsum("prd,pcd->prc", row_set, col_set, preferred_element_type=jnp.float32)
        * score_scale
    )
    masked = jnp.where(inside, scores, NEG)
    row_high = jnp.max(masked, axis=2)
    row_sum = jnp.sum(jnp.where(inside, jnp.exp(masked - row_high[:, :, None]), 0.0), axis=2)
    col_high = jnp.max(masked, axis=1)
    col_sum = jnp.sum(jnp.where(inside, jnp.exp(masked - col_high[:, None, :]), 0.0), axis=1)
    col_stats = jnp.stack([col_high, col_sum])
    col_stats = group_merge(group_merge(col_stats, "dp", 1, 2), "dp", 2, dp_size // 2)
    col_high, col_sum = (col_stats[0], col_stats[1])
    col_lse = jnp.where(col_valid, col_high + jnp.log(jnp.where(col_valid, col_sum, 1.0)), 0.0)
    lanes = jnp.arange(row_count, dtype=jnp.int32)[None, :]
    carried = jnp.where(lanes == 0, own_positive[:, None], 0.0)
    row_stats = jnp.stack([row_high, row_sum, carried])
    row_stats = group_merge(group_merge(row_stats, "pair", 1, 4), "pair", 4, pair_size // 4)
    row_high, row_sum, carried = (row_stats[0], row_stats[1], row_stats[2])
    row_lse = jnp.where(row_valid, row_high + jnp.log(jnp.where(row_valid, row_sum, 1.0)), 0.0)
    row_part = jnp.sum(row_lse, axis=1) - 2.0 * carried[:, 0]
    prob_row = jnp.where(inside, jnp.exp(scores - row_lse[:, :, None]), 0.0)
    prob_col = jnp.where(inside, jnp.exp(scores - col_lse[:, None, :]), 0.0)
    weights = (pair_scale[:, None, None] * 0.5 * (prob_row + prob_col)).astype(jnp.bfloat16)
    weights = lax.optimization_barrier(weights)
    grad_rows = (
        jnp.einsum("prc,pcd->prd", weights, col_set, preferred_element_type=jnp.float32)
        * score_scale
    )
    grad_cols = (
        jnp.einsum("prc,prd->pcd", weights, row_set, preferred_element_type=jnp.float32)
        * score_scale
    )
    anchor_part = lax.psum_scatter(grad_rows, "pair", scatter_dimension=1, tiled=True)
    width_lanes = jnp.arange(model_width, dtype=jnp.int32)[None, :]
    slots = (jnp.arange(pair_count, dtype=jnp.int32) * dp_size + dp_index)[:, None]
    loss_row = jnp.sum(jnp.where(width_lanes == slots, row_part[:, None], 0.0), axis=0)
    extra = jnp.concatenate([loss_row[None], jnp.zeros((7, model_width), jnp.float32)], axis=0)
    partner_part, loss_row = two_stage_reduce_scatter(grad_cols, extra, "dp", dp_size, shard_rows)
    row_parts = loss_row[: pair_count * dp_size].reshape(pair_count, dp_size)
    col_total = butterfly_sum(jnp.sum(col_lse, axis=1), "pair", pair_size)
    totals = col_total + jnp.sum(row_parts, axis=1)
    loss_value = jnp.sum(totals / (2.0 * counts.astype(jnp.float32))) / pair_count
    own_term = (pair_scale * score_scale)[:, None, None]
    keep_rows = own_valid[:, :, None]
    anchor_out = jnp.where(keep_rows, anchor_part - own_term * partner.astype(jnp.float32), 0.0)
    partner_out = jnp.where(keep_rows, partner_part - own_term * anchor.astype(jnp.float32), 0.0)
    return (loss_value, anchor_out, partner_out)


def solution(mesh):
    in_specs = (P(None, ("dp", "pair"), None), P(None, ("dp", "pair"), None), P(), P())
    out_specs = (P(), P(None, ("dp", "pair"), None), P(None, ("dp", "pair"), None))
    return jax.shard_map(
        per_device, mesh=mesh, in_specs=in_specs, out_specs=out_specs, check_vma=False
    )
```

profile of v0, /device:TPU:1, one launch (start us, length us, event | category | flops | bytes accessed | tf_op | source)
XLA Modules:
  0.0 210.4 jit_solution(16853269041058675096)
XLA Ops:
  8.0 2.6 %collective-permute-start = (bf16[5,32,1024]{2,1,0:T(8,128)(2,1)}, bf16[5,32,1024]{2,1,0:T(8,128)(2,1)S(1)}, u32[]{:S(2)}, u32[]{:S(2)}) collective-permute-start(bf16[5,32,1024]{2,1,0:T(8,128)(2,1)} %param.7), channel_id=1, source_target_pairs={{0,16},{16,32},{32,48},{48,64},{64,80},{80,96},{96,112},{112,0},{1... | collective-permute-start | bytes 983048 | tf_op jit(solution)/shard_map/ppermute | solution.py:71
  10.9 1.2 fusion.17
  12.1 0.8 select_reduce_fusion.1
  13.6 1.3 collective-permute-done
  14.9 2.4 %collective-permute-start.1 = (bf16[5,32,1024]{2,1,0:T(8,128)(2,1)S(1)}, bf16[5,32,1024]{2,1,0:T(8,128)(2,1)S(1)}, u32[]{:S(2)}, u32[]{:S(2)}) collective-permute-start(bf16[5,32,1024]{2,1,0:T(8,128)(2,1)S(1)} %collective-permute-done), channel_id=1, source_target_pairs={{0,16},{16,32},{32,48},{48,64},{64,80},{80,96},{96,112},{112,0},{1... | collective-permute-start | bytes 983048 | tf_op jit(solution)/shard_map/ppermute | solution.py:71
  17.3 0.7 broadcast_compare_fusion.1
  18.0 3.3 %collective-permute-done.1 = bf16[5,32,1024]{2,1,0:T(8,128)(2,1)S(1)} collective-permute-done((bf16[5,32,1024]{2,1,0:T(8,128)(2,1)S(1)}, bf16[5,32,1024]{2,1,0:T(8,128)(2,1)S(1)}, u32[]{:S(2)}, u32[]{:S(2)}) %collective-permute-start.1) | collective-permute-done | bytes 327712 | tf_op jit(solution)/shard_map/ppermute | solution.py:71
  21.3 2.5 %collective-permute-start.2 = (bf16[5,32,1024]{2,1,0:T(8,128)(2,1)S(1)}, bf16[5,32,1024]{2,1,0:T(8,128)(2,1)S(1)}, u32[]{:S(2)}, u32[]{:S(2)}) collective-permute-start(bf16[5,32,1024]{2,1,0:T(8,128)(2,1)S(1)} %collective-permute-done.1), channel_id=1, source_target_pairs={{0,16},{16,32},{32,48},{48,64},{64,80},{80,96},{96,112},{112,0},{1... | collective-permute-start | bytes 983048 | tf_op jit(solution)/shard_map/ppermute | solution.py:71
  23.8 0.7 broadcast_compare_fusion
  24.5 1.2 collective-permute-start.5
  25.8 2.0 collective-permute-done.2
  27.8 2.5 %collective-permute-start.3 = (bf16[5,32,1024]{2,1,0:T(8,128)(2,1)S(1)}, bf16[5,32,1024]{2,1,0:T(8,128)(2,1)S(1)}, u32[]{:S(2)}, u32[]{:S(2)}) collective-permute-start(bf16[5,32,1024]{2,1,0:T(8,128)(2,1)S(1)} %collective-permute-done.2), channel_id=1, source_target_pairs={{0,16},{16,32},{32,48},{48,64},{64,80},{80,96},{96,112},{112,0},{1... | collective-permute-start | bytes 983048 | tf_op jit(solution)/shard_map/ppermute | solution.py:71
  30.4 1.0 collective-permute-done.5
  31.4 1.9 collective-permute-start.6
  33.3 1.0 collective-permute-done.3
  34.3 0.8 constant_dynamic-update-slice_fusion.15
  35.1 0.8 constant_dynamic-update-slice_fusion.14
  35.9 0.8 constant_dynamic-update-slice_fusion.13
  36.6 0.7 constant_dynamic-update-slice_fusion.12
  37.4 1.8 constant_dynamic-update-slice_fusion.11
  39.1 0.7 constant_dynamic-update-slice_fusion.10
  39.9 0.8 constant_dynamic-update-slice_fusion.9
  40.7 0.8 constant_dynamic-update-slice_fusion.8
  41.4 0.8 constant_dynamic-update-slice_fusion.7
  42.2 0.8 constant_dynamic-update-slice_fusion.6
  43.0 0.8 constant_dynamic-update-slice_fusion.5
  43.7 0.8 constant_dynamic-update-slice_fusion.4
  44.5 0.8 constant_dynamic-update-slice_fusion.3
  45.3 0.8 constant_dynamic-update-slice_fusion.2
  46.0 0.8 constant_dynamic-update-slice_fusion.1
  46.8 0.7 constant_dynamic-update-slice_fusion
  47.6 22.4 %all-gather.2.cloned.1.call-done = bf16[5,512,1024]{2,1,0:T(8,128)(2,1)} async-done(((bf16[5,32,1024]{2,1,0:T(8,128)(2,1)}), bf16[5,512,1024]{2,1,0:T(8,128)(2,1)}) %all-gather.2.cloned.1.call-update) | async-done | bytes 5242896 | tf_op jit(solution)/shard_map/all_gather | solution.py:120
  69.9 5.2 %fusion.11 = (f32[5,256]{1,0:T(8,128)S(1)}, f32[5,512]{1,0:T(8,128)S(1)}, f32[5,256,512]{2,1,0:T(8,128)S(1)}) fusion(pred[5,256]{1,0:T(8,128)(4,1)S(1)} %broadcast_compare_fusion.1, pred[5,512]{1,0:T(8,128)(4,1)S(1)} %broadcast_compare_fusion, bf16[5,512,1024]{2,1,0:T(8,128)(2,1)} %all-gather.2.cloned.1.call-done, ...), kind=kOutput, calls=%fused_computation.30 | convolution fusion | flops 1345450240 | bytes 10504964 | tf_op jit(solution)/shard_map/prd,pcd->prc/dot_general | solution.py:132
  75.1 1.5 copy-done.2
  76.6 1.9 fusion
  78.6 0.7 collective-permute-start.7
  79.4 0.8 collective-permute-done.7
  80.8 2.5 %collective-permute-start.10 = (f32[2,5,256]{2,1,0:T(8,128)S(1)}, f32[2,5,256]{2,1,0:T(8,128)S(1)}, u32[]{:S(2)}, u32[]{:S(2)}) collective-permute-start(f32[2,5,256]{2,1,0:T(8,128)S(1)} %get-tuple-element.34), channel_id=1, source_target_pairs={{0,96},{16,112},{32,0},{48,16},{64,32},{80,48},{96,64},{112,80},{1... | collective-permute-start | bytes 30728 | tf_op jit(solution)/shard_map/ppermute | solution.py:37
  84.5 2.5 %collective-permute-start.17 = (f32[3,5,512]{2,0,1:T(4,128)S(1)}, f32[3,5,512]{2,0,1:T(4,128)S(1)}, u32[]{:S(2)}, u32[]{:S(2)}) collective-permute-start(f32[3,5,512]{2,0,1:T(4,128)S(1)} %get-tuple-element.32), channel_id=1, source_target_pairs={{0,3},{1,0},{2,1},{3,2},{4,7},{5,4},{6,5},{7,6},{8,11},{9,8},{10,9... | collective-permute-start | bytes 92168 | tf_op jit(solution)/shard_map/ppermute | solution.py:37
  88.8 2.6 %collective-permute-done.16 = f32[3,5,512]{2,0,1:T(4,128)S(1)} collective-permute-done((f32[3,5,512]{2,0,1:T(4,128)S(1)}, f32[3,5,512]{2,0,1:T(4,128)S(1)}, u32[]{:S(2)}, u32[]{:S(2)}) %collective-permute-start.16) | collective-permute-done | bytes 30752 | tf_op jit(solution)/shard_map/ppermute | solution.py:37
  92.8 1.1 collective-permute-start.20
  95.8 2.5 %collective-permute-done.19 = f32[3,5,512]{2,0,1:T(4,128)S(1)} collective-permute-done((f32[3,5,512]{2,0,1:T(4,128)S(1)}, f32[3,5,512]{2,0,1:T(4,128)S(1)}, u32[]{:S(2)}, u32[]{:S(2)}) %collective-permute-start.19) | collective-permute-done | bytes 30752 | tf_op jit(solution)/shard_map/ppermute | solution.py:37
  99.8 2.7 %fusion.4 = bf16[5,512,256]{1,2,0:T(8,128)(2,1)S(1)} fusion(f32[5,256,512]{2,1,0:T(8,128)} %copy-done.2, f32[5,256]{1,0:T(8,128)S(1)} %get-tuple-element.9, f32[5,512]{1,0:T(8,128)S(1)} %get-tuple-element.13, f32[5]{0:T(128)S(1)} %get-tuple-element.40, pred[5,256]{1,0:T(8,128)(4,1)S(1)} %broadcast_compare_fusion.1, pred[5,512]{1,0:T(8,128)(4,1)S(1)} %broadcast_compare_fusion), kind=kLoop, calls=%fused_computation.15 | loop fusion | flops 5898240 | bytes 3951380 | tf_op jit(solution)/shard_map/convert_element_type | solution.py:153
  102.5 7.3 %broadcast_multiply_fusion = f32[5,512,1024]{2,1,0:T(8,128)} fusion(bf16[5,512,256]{1,2,0:T(8,128)(2,1)S(1)} %fusion.4, bf16[5,512,1024]{2,1,0:T(8,128)(2,1)} %constant_dynamic-update-slice_fusion, s32[]{:T(128)S(6)} %select_n.293), kind=kOutput, calls=%fused_computation.9 | convolution fusion | flops 1344798720 | bytes 14417924 | tf_op jit(solution)/shard_map/prc,pcd->prd/dot_general | solution.py:156
  110.2 4.0 %broadcast_multiply_fusion.1 = f32[5,256,1024]{2,1,0:T(8,128)S(1)} fusion(bf16[5,512,256]{1,2,0:T(8,128)(2,1)S(1)} %fusion.4, bf16[5,512,1024]{2,1,0:T(8,128)(2,1)} %all-gather.2.cloned.1.call-done), kind=kOutput, calls=%fused_computation.21 | convolution fusion | flops 1343488000 | bytes 11796480 | tf_op jit(solution)/shard_map/prc,prd->pcd/dot_general | solution.py:160
  114.5 2.0 maximum_maximum_fusion
  116.5 0.8 copy-done
  117.4 4.4 %collective-permute-start.21 = (f32[648,1024]{1,0:T(8,128)}, f32[648,1024]{1,0:T(8,128)}, u32[]{:S(2)}, u32[]{:S(2)}) collective-permute-start(f32[648,1024]{1,0:T(8,128)} %maximum_maximum_fusion), channel_id=1, source_target_pairs={{0,16},{16,0},{32,48},{48,32},{64,80},{80,64},{96,112},{112,96},{1... | collective-permute-start | bytes 7962632 | tf_op jit(solution)/shard_map/ppermute | solution.py:89
  121.8 4.9 %collective-permute-done.21 = f32[648,1024]{1,0:T(8,128)} collective-permute-done((f32[648,1024]{1,0:T(8,128)}, f32[648,1024]{1,0:T(8,128)}, u32[]{:S(2)}, u32[]{:S(2)}) %collective-permute-start.21) | collective-permute-done | bytes 2654240 | tf_op jit(solution)/shard_map/ppermute | solution.py:89
  126.7 2.1 %slice.312 = f32[640,1024]{1,0:T(8,128)S(1)} slice(f32[648,1024]{1,0:T(8,128)} %collective-permute-done.21), slice={[0:640], [0:1024]} | slice | bytes 5242880 | tf_op jit(solution)/shard_map/slice | solution.py:90
  128.8 0.8 bitcast_add_fusion
  129.8 0.8 slice_add_fusion
  130.7 1.6 collective-permute-start.22
  132.2 16.5 %collective-permute-done.22 = f32[168,1024]{1,0:T(8,128)S(1)} collective-permute-done((f32[168,1024]{1,0:T(8,128)S(1)}, f32[168,1024]{1,0:T(8,128)S(1)}, u32[]{:S(2)}, u32[]{:S(2)}) %collective-permute-start.22) | collective-permute-done | bytes 688160 | tf_op jit(solution)/shard_map/ppermute | solution.py:102
  149.1 16.8 %collective-permute-done.23 = f32[168,1024]{1,0:T(8,128)S(1)} collective-permute-done((f32[168,1024]{1,0:T(8,128)S(1)}, f32[168,1024]{1,0:T(8,128)S(1)}, u32[]{:S(2)}, u32[]{:S(2)}) %collective-permute-start.23) | collective-permute-done | bytes 688160 | tf_op jit(solution)/shard_map/ppermute | solution.py:102
  165.9 0.9 fusion.13
  167.0 2.8 %collective-permute-done.11 = f32[5]{0:T(128)S(1)} collective-permute-done((f32[5]{0:T(128)S(1)}, f32[5]{0:T(128)S(1)}, u32[]{:S(2)}, u32[]{:S(2)}) %collective-permute-start.11) | collective-permute-done | bytes 52 | tf_op jit(solution)/shard_map/ppermute | solution.py:50
  169.8 1.0 collective-permute-start.12
  170.8 2.9 %collective-permute-done.12 = f32[5]{0:T(128)S(1)} collective-permute-done((f32[5]{0:T(128)S(1)}, f32[5]{0:T(128)S(1)}, u32[]{:S(2)}, u32[]{:S(2)}) %collective-permute-start.12) | collective-permute-done | bytes 52 | tf_op jit(solution)/shard_map/ppermute | solution.py:50
  173.7 2.7 %collective-permute-done.13 = f32[5]{0:T(128)S(1)} collective-permute-done((f32[5]{0:T(128)S(1)}, f32[5]{0:T(128)S(1)}, u32[]{:S(2)}, u32[]{:S(2)}) %collective-permute-start.13) | collective-permute-done | bytes 52 | tf_op jit(solution)/shard_map/ppermute | solution.py:50
  176.3 1.3 collective-permute-start.14
  177.6 5.5 %collective-permute-done.24 = f32[168,1024]{1,0:T(8,128)S(1)} collective-permute-done((f32[168,1024]{1,0:T(8,128)}, f32[168,1024]{1,0:T(8,128)S(1)}, u32[]{:S(2)}, u32[]{:S(2)}) %collective-permute-start.24) | collective-permute-done | bytes 688160 | tf_op jit(solution)/shard_map/ppermute | solution.py:102
  184.8 15.2 %reduce-scatter.2.cloned.1.call-done = f32[5,32,1024]{2,1,0:T(8,128)} async-done(((f32[5,512,1024]{2,1,0:T(8,128)}), f32[5,32,1024]{2,1,0:T(8,128)}) %reduce-scatter.2.cloned.1.call-update) | async-done | bytes 655376 | tf_op jit(solution)/shard_map/reduce_scatter | solution.py:163
  200.1 2.4 %fusion.16 = (f32[5,32,1024]{2,1,0:T(8,128)}, f32[5,32,1024]{2,1,0:T(8,128)}) fusion(f32[5,32,1024]{2,1,0:T(8,128)S(1)} %bitcast.353, bf16[5,32,1024]{2,1,0:T(8,128)(2,1)S(1)} %copy-done.4, f32[5]{0:T(128)S(1)} %get-tuple-element.39, pred[5,32]{1,0:T(8,128)(4,1)S(1)} %broadcast_compare_fusion.2, f32[5,32,1024]{2,1,0:T(8,128)} %reduce-scatter.2.cloned.1.call-done, ...), kind=kLoop, calls=%fused_computation.38 | loop fusion | flops 1310720 | bytes 3276980 | tf_op jit(solution)/shard_map/jit(_where)/select_n | solution.py:176
  (99 shorter events, 12.5 us)
Async XLA Ops:
  7.2 37.4 %copy-start.3 = (bf16[5,32,1024]{2,1,0:T(8,128)(2,1)S(1)}, bf16[5,32,1024]{2,1,0:T(8,128)(2,1)}, u32[]{:S(2)}) copy-start(bf16[5,32,1024]{2,1,0:T(8,128)(2,1)} %param.7) | copy-start | bytes 983044
  7.2 62.7 %all-gather.2.cloned.1.call-start = ((), (), s32[]{:S(2)}) async-start(), calls=%async_computation.1 | async-start | bytes 5570560 | tf_op jit(solution)/shard_map/all_gather | solution.py:120
  7.9 192.2 %reduce-scatter.2.cloned.1.call-start = ((), (), s32[]{:S(2)}) async-start(), calls=%async_computation.2 | async-start | bytes 11141120 | tf_op jit(solution)/shard_map/reduce_scatter | solution.py:163
  8.0 6.9 %collective-permute-start = (bf16[5,32,1024]{2,1,0:T(8,128)(2,1)}, bf16[5,32,1024]{2,1,0:T(8,128)(2,1)S(1)}, u32[]{:S(2)}, u32[]{:S(2)}) collective-permute-start(bf16[5,32,1024]{2,1,0:T(8,128)(2,1)} %param.7), channel_id=1, source_target_pairs={{0,16},{16,32},{32,48},{48,64},{64,80},{80,96},{96,112},{112,0},{1... | collective-permute-start | bytes 983048 | tf_op jit(solution)/shard_map/ppermute | solution.py:71
  10.6 13.9 %collective-permute-start.4 = (bf16[5,32,1024]{2,1,0:T(8,128)(2,1)}, bf16[5,32,1024]{2,1,0:T(8,128)(2,1)S(1)}, u32[]{:S(2)}, u32[]{:S(2)}) collective-permute-start(bf16[5,32,1024]{2,1,0:T(8,128)(2,1)} %param.7), channel_id=1, source_target_pairs={{0,112},{16,0},{32,16},{48,32},{64,48},{80,64},{96,80},{112,96},{1... | collective-permute-start | bytes 983048 | tf_op jit(solution)/shard_map/ppermute | solution.py:74
  14.9 6.4 %collective-permute-start.1 = (bf16[5,32,1024]{2,1,0:T(8,128)(2,1)S(1)}, bf16[5,32,1024]{2,1,0:T(8,128)(2,1)S(1)}, u32[]{:S(2)}, u32[]{:S(2)}) collective-permute-start(bf16[5,32,1024]{2,1,0:T(8,128)(2,1)S(1)} %collective-permute-done), channel_id=1, source_target_pairs={{0,16},{16,32},{32,48},{48,64},{64,80},{80,96},{96,112},{112,0},{1... | collective-permute-start | bytes 983048 | tf_op jit(solution)/shard_map/ppermute | solution.py:71
  21.3 6.5 %collective-permute-start.2 = (bf16[5,32,1024]{2,1,0:T(8,128)(2,1)S(1)}, bf16[5,32,1024]{2,1,0:T(8,128)(2,1)S(1)}, u32[]{:S(2)}, u32[]{:S(2)}) collective-permute-start(bf16[5,32,1024]{2,1,0:T(8,128)(2,1)S(1)} %collective-permute-done.1), channel_id=1, source_target_pairs={{0,16},{16,32},{32,48},{48,64},{64,80},{80,96},{96,112},{112,0},{1... | collective-permute-start | bytes 983048 | tf_op jit(solution)/shard_map/ppermute | solution.py:71
  24.5 6.9 %collective-permute-start.5 = (bf16[5,32,1024]{2,1,0:T(8,128)(2,1)S(1)}, bf16[5,32,1024]{2,1,0:T(8,128)(2,1)S(1)}, u32[]{:S(2)}, u32[]{:S(2)}) collective-permute-start(bf16[5,32,1024]{2,1,0:T(8,128)(2,1)S(1)} %collective-permute-done.4), channel_id=1, source_target_pairs={{0,112},{16,0},{32,16},{48,32},{64,48},{80,64},{96,80},{112,96},{1... | collective-permute-start | bytes 983048 | tf_op jit(solution)/shard_map/ppermute | solution.py:74
  27.8 6.5 %collective-permute-start.3 = (bf16[5,32,1024]{2,1,0:T(8,128)(2,1)S(1)}, bf16[5,32,1024]{2,1,0:T(8,128)(2,1)S(1)}, u32[]{:S(2)}, u32[]{:S(2)}) collective-permute-start(bf16[5,32,1024]{2,1,0:T(8,128)(2,1)S(1)} %collective-permute-done.2), channel_id=1, source_target_pairs={{0,16},{16,32},{32,48},{48,64},{64,80},{80,96},{96,112},{112,0},{1... | collective-permute-start | bytes 983048 | tf_op jit(solution)/shard_map/ppermute | solution.py:71
  31.4 9.3 %collective-permute-start.6 = (bf16[5,32,1024]{2,1,0:T(8,128)(2,1)S(1)}, bf16[5,32,1024]{2,1,0:T(8,128)(2,1)S(1)}, u32[]{:S(2)}, u32[]{:S(2)}) collective-permute-start(bf16[5,32,1024]{2,1,0:T(8,128)(2,1)S(1)} %collective-permute-done.5), channel_id=1, source_target_pairs={{0,112},{16,0},{32,16},{48,32},{64,48},{80,64},{96,80},{112,96},{1... | collective-permute-start | bytes 983048 | tf_op jit(solution)/shard_map/ppermute | solution.py:74
  47.6 47.4 %copy-start.5 = (s32[5]{0:T(128)S(1)}, s32[5]{0:T(128)}, u32[]{:S(2)}) copy-start(s32[5]{0:T(128)} %param.8) | copy-start | bytes 64
  75.1 1.5 copy-start.2
  78.6 1.6 collective-permute-start.7
  80.8 6.7 %collective-permute-start.10 = (f32[2,5,256]{2,1,0:T(8,128)S(1)}, f32[2,5,256]{2,1,0:T(8,128)S(1)}, u32[]{:S(2)}, u32[]{:S(2)}) collective-permute-start(f32[2,5,256]{2,1,0:T(8,128)S(1)} %get-tuple-element.34), channel_id=1, source_target_pairs={{0,96},{16,112},{32,0},{48,16},{64,32},{80,48},{96,64},{112,80},{1... | collective-permute-start | bytes 30728 | tf_op jit(solution)/shard_map/ppermute | solution.py:37
  83.3 4.8 %collective-permute-start.9 = (f32[2,5,256]{2,1,0:T(8,128)S(1)}, f32[2,5,256]{2,1,0:T(8,128)S(1)}, u32[]{:S(2)}, u32[]{:S(2)}) collective-permute-start(f32[2,5,256]{2,1,0:T(8,128)S(1)} %get-tuple-element.34), channel_id=1, source_target_pairs={{0,64},{16,80},{32,96},{48,112},{64,0},{80,16},{96,32},{112,48},{1... | collective-permute-start | bytes 30728 | tf_op jit(solution)/shard_map/ppermute | solution.py:37
  83.9 4.3 %collective-permute-start.8 = (f32[2,5,256]{2,1,0:T(8,128)S(1)}, f32[2,5,256]{2,1,0:T(8,128)S(1)}, u32[]{:S(2)}, u32[]{:S(2)}) collective-permute-start(f32[2,5,256]{2,1,0:T(8,128)S(1)} %get-tuple-element.34), channel_id=1, source_target_pairs={{0,32},{16,48},{32,64},{48,80},{64,96},{80,112},{96,0},{112,16},{1... | collective-permute-start | bytes 30728 | tf_op jit(solution)/shard_map/ppermute | solution.py:37
  84.5 4.3 %collective-permute-start.17 = (f32[3,5,512]{2,0,1:T(4,128)S(1)}, f32[3,5,512]{2,0,1:T(4,128)S(1)}, u32[]{:S(2)}, u32[]{:S(2)}) collective-permute-start(f32[3,5,512]{2,0,1:T(4,128)S(1)} %get-tuple-element.32), channel_id=1, source_target_pairs={{0,3},{1,0},{2,1},{3,2},{4,7},{5,4},{6,5},{7,6},{8,11},{9,8},{10,9... | collective-permute-start | bytes 92168 | tf_op jit(solution)/shard_map/ppermute | solution.py:37
  87.0 4.4 %collective-permute-start.16 = (f32[3,5,512]{2,0,1:T(4,128)S(1)}, f32[3,5,512]{2,0,1:T(4,128)S(1)}, u32[]{:S(2)}, u32[]{:S(2)}) collective-permute-start(f32[3,5,512]{2,0,1:T(4,128)S(1)} %get-tuple-element.32), channel_id=1, source_target_pairs={{0,2},{1,3},{2,0},{3,1},{4,6},{5,7},{6,4},{7,5},{8,10},{9,11},{10,... | collective-permute-start | bytes 92168 | tf_op jit(solution)/shard_map/ppermute | solution.py:37
  87.6 4.3 %collective-permute-start.15 = (f32[3,5,512]{2,0,1:T(4,128)S(1)}, f32[3,5,512]{2,0,1:T(4,128)S(1)}, u32[]{:S(2)}, u32[]{:S(2)}) collective-permute-start(f32[3,5,512]{2,0,1:T(4,128)S(1)} %get-tuple-element.32), channel_id=1, source_target_pairs={{0,1},{1,2},{2,3},{3,0},{4,5},{5,6},{6,7},{7,4},{8,9},{9,10},{10,1... | collective-permute-start | bytes 92168 | tf_op jit(solution)/shard_map/ppermute | solution.py:37
  92.8 2.9 %collective-permute-start.20 = (f32[3,5,512]{2,0,1:T(4,128)S(1)}, f32[3,5,512]{2,0,1:T(4,128)S(1)}, u32[]{:S(2)}, u32[]{:S(2)}) collective-permute-start(f32[3,5,512]{2,0,1:T(4,128)S(1)} %get-tuple-element.30), channel_id=1, source_target_pairs={{0,12},{1,13},{2,14},{3,15},{4,0},{5,1},{6,2},{7,3},{8,4},{9,5},{1... | collective-permute-start | bytes 92168 | tf_op jit(solution)/shard_map/ppermute | solution.py:37
  93.9 4.4 %collective-permute-start.19 = (f32[3,5,512]{2,0,1:T(4,128)S(1)}, f32[3,5,512]{2,0,1:T(4,128)S(1)}, u32[]{:S(2)}, u32[]{:S(2)}) collective-permute-start(f32[3,5,512]{2,0,1:T(4,128)S(1)} %get-tuple-element.30), channel_id=1, source_target_pairs={{0,8},{1,9},{2,10},{3,11},{4,12},{5,13},{6,14},{7,15},{8,0},{9,1},... | collective-permute-start | bytes 92168 | tf_op jit(solution)/shard_map/ppermute | solution.py:37
  94.6 4.1 %collective-permute-start.18 = (f32[3,5,512]{2,0,1:T(4,128)S(1)}, f32[3,5,512]{2,0,1:T(4,128)S(1)}, u32[]{:S(2)}, u32[]{:S(2)}) collective-permute-start(f32[3,5,512]{2,0,1:T(4,128)S(1)} %get-tuple-element.30), channel_id=1, source_target_pairs={{0,4},{1,5},{2,6},{3,7},{4,8},{5,9},{6,10},{7,11},{8,12},{9,13},{1... | collective-permute-start | bytes 92168 | tf_op jit(solution)/shard_map/ppermute | solution.py:37
  114.3 3.1 %copy-start = (f32[5,256,1024]{2,1,0:T(8,128)}, f32[5,256,1024]{2,1,0:T(8,128)S(1)}, u32[]{:S(2)}) copy-start(f32[5,256,1024]{2,1,0:T(8,128)S(1)} %broadcast_multiply_fusion.1) | copy-start | bytes 15728644
  117.4 9.4 %collective-permute-start.21 = (f32[648,1024]{1,0:T(8,128)}, f32[648,1024]{1,0:T(8,128)}, u32[]{:S(2)}, u32[]{:S(2)}) collective-permute-start(f32[648,1024]{1,0:T(8,128)} %maximum_maximum_fusion), channel_id=1, source_target_pairs={{0,16},{16,0},{32,48},{48,32},{64,80},{80,64},{96,112},{112,96},{1... | collective-permute-start | bytes 7962632 | tf_op jit(solution)/shard_map/ppermute | solution.py:89
  121.8 7.0 %copy-start.1 = (f32[5,256,1024]{2,1,0:T(8,128)S(1)}, f32[5,256,1024]{2,1,0:T(8,128)}, u32[]{:S(2)}) copy-start(f32[5,256,1024]{2,1,0:T(8,128)} %copy-done) | copy-start | bytes 15728644
  129.8 70.3 %copy-start.4 = (bf16[5,32,1024]{2,1,0:T(8,128)(2,1)S(1)}, bf16[5,32,1024]{2,1,0:T(8,128)(2,1)}, u32[]{:S(2)}) copy-start(bf16[5,32,1024]{2,1,0:T(8,128)(2,1)} %param.6) | copy-start | bytes 983044
  130.7 18.0 %collective-permute-start.22 = (f32[168,1024]{1,0:T(8,128)S(1)}, f32[168,1024]{1,0:T(8,128)S(1)}, u32[]{:S(2)}, u32[]{:S(2)}) collective-permute-start(f32[168,1024]{1,0:T(8,128)S(1)} %pad_maximum_fusion.3), channel_id=1, source_target_pairs={{0,32},{16,48},{32,64},{48,80},{64,96},{80,112},{96,0},{112,16},{1... | collective-permute-start | bytes 2064392 | tf_op jit(solution)/shard_map/ppermute | solution.py:102
  148.8 17.1 %collective-permute-start.23 = (f32[168,1024]{1,0:T(8,128)S(1)}, f32[168,1024]{1,0:T(8,128)S(1)}, u32[]{:S(2)}, u32[]{:S(2)}) collective-permute-start(f32[168,1024]{1,0:T(8,128)S(1)} %fusion.12), channel_id=1, source_target_pairs={{0,32},{16,48},{32,64},{48,80},{64,96},{80,112},{96,0},{112,16},{1... | collective-permute-start | bytes 2064392 | tf_op jit(solution)/shard_map/ppermute | solution.py:102
  166.9 16.3 %collective-permute-start.24 = (f32[168,1024]{1,0:T(8,128)}, f32[168,1024]{1,0:T(8,128)S(1)}, u32[]{:S(2)}, u32[]{:S(2)}) collective-permute-start(f32[168,1024]{1,0:T(8,128)} %fusion.13), channel_id=1, source_target_pairs={{0,32},{16,48},{32,64},{48,80},{64,96},{80,112},{96,0},{112,16},{1... | collective-permute-start | bytes 2064392 | tf_op jit(solution)/shard_map/ppermute | solution.py:102
  166.9 2.8 %collective-permute-start.11 = (f32[5]{0:T(128)S(1)}, f32[5]{0:T(128)S(1)}, u32[]{:S(2)}, u32[]{:S(2)}) collective-permute-start(f32[5]{0:T(128)S(1)} %get-tuple-element.8), channel_id=1, source_target_pairs={{0,1},{1,0},{2,3},{3,2},{4,5},{5,4},{6,7},{7,6},{8,9},{9,8},{10,11... | collective-permute-start | bytes 68 | tf_op jit(solution)/shard_map/ppermute | solution.py:50
  169.8 3.9 %collective-permute-start.12 = (f32[5]{0:T(128)S(1)}, f32[5]{0:T(128)S(1)}, u32[]{:S(2)}, u32[]{:S(2)}) collective-permute-start(f32[5]{0:T(128)S(1)} %fusion.90), channel_id=1, source_target_pairs={{0,2},{1,3},{2,0},{3,1},{4,6},{5,7},{6,4},{7,5},{8,10},{9,11},{10,... | collective-permute-start | bytes 68 | tf_op jit(solution)/shard_map/ppermute | solution.py:50
  173.7 2.7 %collective-permute-start.13 = (f32[5]{0:T(128)S(1)}, f32[5]{0:T(128)S(1)}, u32[]{:S(2)}, u32[]{:S(2)}) collective-permute-start(f32[5]{0:T(128)S(1)} %fusion.89), channel_id=1, source_target_pairs={{0,4},{1,5},{2,6},{3,7},{4,0},{5,1},{6,2},{7,3},{8,12},{9,13},{10,... | collective-permute-start | bytes 68 | tf_op jit(solution)/shard_map/ppermute | solution.py:50
  176.3 7.2 %collective-permute-start.14 = (f32[5]{0:T(128)S(1)}, f32[5]{0:T(128)S(1)}, u32[]{:S(2)}, u32[]{:S(2)}) collective-permute-start(f32[5]{0:T(128)S(1)} %fusion.88), channel_id=1, source_target_pairs={{0,8},{1,9},{2,10},{3,11},{4,12},{5,13},{6,14},{7,15},{8,0},{9,1},... | collective-permute-start | bytes 68 | tf_op jit(solution)/shard_map/ppermute | solution.py:50
Sparse Core Ops, SparseCore 0:
  10.2 59.7 all-gather.1
  110.0 90.0 reduce-scatter.1
where the time goes:
time: 211 us; the launch traced here: 210 us
  waiting for transfers between devices  106 us (50%)
  starting transfers between devices  32.1 us (15%)
  local copies, waits for them, and re-layouts  20.9 us (10%)
  other arithmetic  18.4 us (9%)
  matrix products  16.5 us (8%)
  between operations  16.2 us (8%)
    ppermute x3, waiting for transfers between devices, two_stage_reduce_scatter(): running = lax.ppermute(running, axis, ring) + addend(chip - 1 - step)  38.8 us
    all_gather x1, waiting for transfers between devices, per_device(): row_set = lax.all_gather(anchor, 'pair', axis=1, tiled=True)  22.4 us
    reduce_scatter x1, waiting for transfers between devices, per_device(): lax.psum_scatter(grad_rows, 'pair', scatter_dimension=1, tiled=True)  15.2 us
    unnamed x28, local copies, waits for them, and re-layouts  14.9 us
    ppermute x10, starting transfers between devices, group_merge(): received.append(lax.ppermute(stats, axis, perm))  10.2 us
    ppermute x4, starting transfers between devices, ring_gather(): ahead = lax.ppermute(ahead, axis, forward)  9.95 us
    ppermute x4, waiting for transfers between devices, butterfly_sum(): other = lax.ppermute(values, axis, [(i, i ^ bit) for i in range(size)])  8.33 us
    ppermute x4, waiting for transfers between devices, ring_gather(): ahead = lax.ppermute(ahead, axis, forward)  7.61 us
  transfers between devices with their start and end apart: 27, of which 20 were waited for; matrix products, arithmetic and copies ran while one was open for 15% of the time, Pallas kernels for 0%

commit v1 on v0

--- a/solution.py
+++ b/solution.py
@@ -1,10 +1,25 @@
+import functools
 import math
 import jax
 import jax.numpy as jnp
 from jax import lax
 from jax.sharding import PartitionSpec as P
+from jax.lax import all_to_all, axis_size
 
 NEG = -1e30
+
+
+def point_the_pipes(arr_in, array_axis):
+    state_next = jnp.concatenate(
+        all_to_all(
+            jnp.stack(axis_size("pair") * [arr_in]), axis_name="pair", split_axis=0, concat_axis=0
+        ),
+        axis=array_axis,
+    )
+    return state_next
+
+
+return_all_counts_on = functools.partial(point_the_pipes, array_axis=1)
 
 
 def merge_pair(mine, other):
@@ -117,7 +132,7 @@
         jnp.sum(anchor.astype(jnp.float32) * partner.astype(jnp.float32), axis=2) * score_scale
     )
     own_positive = jnp.sum(jnp.where(own_valid, positive, 0.0), axis=1)
-    row_set = lax.all_gather(anchor, "pair", axis=1, tiled=True)
+    row_set = return_all_counts_on(anchor)
     col_set = jnp.concatenate(ring_gather(partner, "dp", dp_size), axis=1)
     col_set = jnp.roll(col_set, (dp_index - dp_size // 2) * shard_rows, axis=1)
     row_count = row_set.shape[1]

time: 211 us -> 244 us (1.16)
  starting transfers between devices: 32.1 us -> 48.9 us
  waiting for transfers between devices: 106 us -> 120 us
  local copies, waits for them, and re-layouts: 20.9 us -> 26.8 us
  other arithmetic: 18.4 us -> 13.8 us
    all_to_all x0 -> x1, waiting for transfers between devices: none -> 38.1 us  [point_the_pipes(): all_to_all(jnp.stack(axis_size('pair') * [arr_in]), axis_name='pair', spl...]
    all_gather x1 -> x0, waiting for transfers between devices: 22.4 us -> none  [per_device(): row_set = lax.all_gather(anchor, 'pair', axis=1, tiled=True)]
    all_to_all x0 -> x1, starting transfers between devices: none -> 8.79 us  [point_the_pipes(): all_to_all(jnp.stack(axis_size('pair') * [arr_in]), axis_name='pair', spl...]
    ppermute x10, starting transfers between devices: 10.2 us -> 15.7 us  [group_merge(): received.append(lax.ppermute(stats, axis, perm))]
    ppermute x3, starting transfers between devices: 3.18 us -> 8.22 us  [ring_gather(): behind = lax.ppermute(behind, axis, backward)]
    another operation x0 -> x1, local copies, waits for them, and re-layouts: none -> 3.99 us  [point_the_pipes(): jnp.stack(axis_size('pair') * [arr_in])]
    ppermute x10, waiting for transfers between devices: 7.35 us -> 3.45 us  [group_merge(): received.append(lax.ppermute(stats, axis, perm))]
    reshape x0 -> x1, local copies, waits for them, and re-layouts: none -> 3.12 us  [point_the_pipes(): jnp.concatenate(all_to_all(jnp.stack(axis_size('pair') * [arr_in]), axis_...]
  transfers between devices with their start and end apart: 27 -> 27, of which waited for: 20 -> 19; matrix products, arithmetic and copies ran while one was open for 15% -> 10% of each run, Pallas kernels for 0% -> 0%
where the time goes in v1:
time: 244 us; the launch traced here: 243 us
  waiting for transfers between devices  120 us (49%)
  starting transfers between devices  48.9 us (20%)
  local copies, waits for them, and re-layouts  26.8 us (11%)
  matrix products  16.9 us (7%)
  between operations  16.3 us (7%)
  other arithmetic  13.8 us (6%)
    ppermute x3, waiting for transfers between devices, two_stage_reduce_scatter(): running = lax.ppermute(running, axis, ring) + addend(chip - 1 - step)  38.8 us
    all_to_all x1, waiting for transfers between devices, point_the_pipes(): all_to_all(jnp.stack(axis_size('pair') * [arr_in]), axis_name='pair', spl...  38.1 us
    reduce_scatter x1, waiting for transfers between devices, per_device(): lax.psum_scatter(grad_rows, 'pair', scatter_dimension=1, tiled=True)  16.8 us
    ppermute x10, starting transfers between devices, group_merge(): received.append(lax.ppermute(stats, axis, perm))  15.7 us
    unnamed x32, local copies, waits for them, and re-layouts  13.7 us
    ppermute x4, waiting for transfers between devices, ring_gather(): ahead = lax.ppermute(ahead, axis, forward)  9.33 us
    all_to_all x1, starting transfers between devices, point_the_pipes(): all_to_all(jnp.stack(axis_size('pair') * [arr_in]), axis_name='pair', spl...  8.79 us
    ppermute x4, waiting for transfers between devices, butterfly_sum(): other = lax.ppermute(values, axis, [(i, i ^ bit) for i in range(size)])  8.62 us
  transfers between devices with their start and end apart: 27, of which 19 were waited for; matrix products, arithmetic and copies ran while one was open for 10% of the time, Pallas kernels for 0%

profile of v1, /device:TPU:1, one launch (start us, length us, event | category | flops | bytes accessed | tf_op | source)
XLA Modules:
  0.0 243.2 jit_solution(3293816412200358991)
XLA Ops:
  7.2 4.0 %stack.92 = bf16[16,5,32,1024]{3,2,1,0:T(8,128)(2,1)} broadcast(bf16[5,32,1024]{2,1,0:T(8,128)(2,1)} %param.6), dimensions={1,2,3} | broadcast | bytes 5570560 | tf_op jit(solution)/shard_map/stack | solution.py:15
  11.2 8.8 %all-to-all-start = ((bf16[16,5,32,1024]{3,2,1,0:T(8,128)(2,1)}), bf16[16,5,32,1024]{3,2,1,0:T(8,128)(2,1)}, u32[]{:S(2)}, u32[]{:S(2)}) async-start(bf16[16,5,32,1024]{3,2,1,0:T(8,128)(2,1)} %stack.92), calls=%async_computation | async-start | bytes 10485760 | tf_op jit(solution)/shard_map/all_to_all | solution.py:14
  20.0 1.0 collective-permute-start.4
  21.0 1.1 collective-permute-start
  22.8 3.3 %collective-permute-done = bf16[5,32,1024]{2,1,0:T(8,128)(2,1)S(1)} collective-permute-done((bf16[5,32,1024]{2,1,0:T(8,128)(2,1)S(1)}, bf16[5,32,1024]{2,1,0:T(8,128)(2,1)S(1)}, u32[]{:S(2)}, u32[]{:S(2)}) %collective-permute-start) | collective-permute-done | bytes 327712 | tf_op jit(solution)/shard_map/ppermute | solution.py:86
  26.1 2.5 %collective-permute-start.1 = (bf16[5,32,1024]{2,1,0:T(8,128)(2,1)S(1)}, bf16[5,32,1024]{2,1,0:T(8,128)(2,1)S(1)}, u32[]{:S(2)}, u32[]{:S(2)}) collective-permute-start(bf16[5,32,1024]{2,1,0:T(8,128)(2,1)S(1)} %collective-permute-done), channel_id=1, source_target_pairs={{0,16},{16,32},{32,48},{48,64},{64,80},{80,96},{96,112},{112,0},{1... | collective-permute-start | bytes 983048 | tf_op jit(solution)/shard_map/ppermute | solution.py:86
  28.7 3.9 %collective-permute-done.1 = bf16[5,32,1024]{2,1,0:T(8,128)(2,1)S(1)} collective-permute-done((bf16[5,32,1024]{2,1,0:T(8,128)(2,1)S(1)}, bf16[5,32,1024]{2,1,0:T(8,128)(2,1)S(1)}, u32[]{:S(2)}, u32[]{:S(2)}) %collective-permute-start.1) | collective-permute-done | bytes 327712 | tf_op jit(solution)/shard_map/ppermute | solution.py:86
  32.6 2.5 %collective-permute-start.2 = (bf16[5,32,1024]{2,1,0:T(8,128)(2,1)S(1)}, bf16[5,32,1024]{2,1,0:T(8,128)(2,1)S(1)}, u32[]{:S(2)}, u32[]{:S(2)}) collective-permute-start(bf16[5,32,1024]{2,1,0:T(8,128)(2,1)S(1)} %collective-permute-done.1), channel_id=1, source_target_pairs={{0,16},{16,32},{32,48},{48,64},{64,80},{80,96},{96,112},{112,0},{1... | collective-permute-start | bytes 983048 | tf_op jit(solution)/shard_map/ppermute | solution.py:86
  35.2 3.2 %collective-permute-start.5 = (bf16[5,32,1024]{2,1,0:T(8,128)(2,1)S(1)}, bf16[5,32,1024]{2,1,0:T(8,128)(2,1)S(1)}, u32[]{:S(2)}, u32[]{:S(2)}) collective-permute-start(bf16[5,32,1024]{2,1,0:T(8,128)(2,1)S(1)} %collective-permute-done.4), channel_id=1, source_target_pairs={{0,112},{16,0},{32,16},{48,32},{64,48},{80,64},{96,80},{112,96},{1... | collective-permute-start | bytes 983048 | tf_op jit(solution)/shard_map/ppermute | solution.py:89
  38.4 1.0 collective-permute-done.2
  39.4 2.2 collective-permute-start.3
  42.1 4.0 %collective-permute-start.6 = (bf16[5,32,1024]{2,1,0:T(8,128)(2,1)S(1)}, bf16[5,32,1024]{2,1,0:T(8,128)(2,1)S(1)}, u32[]{:S(2)}, u32[]{:S(2)}) collective-permute-start(bf16[5,32,1024]{2,1,0:T(8,128)(2,1)S(1)} %collective-permute-done.5), channel_id=1, source_target_pairs={{0,112},{16,0},{32,16},{48,32},{64,48},{80,64},{96,80},{112,96},{1... | collective-permute-start | bytes 983048 | tf_op jit(solution)/shard_map/ppermute | solution.py:89
  46.1 1.0 collective-permute-done.3
  47.2 0.8 constant_dynamic-update-slice_fusion.15
  47.9 0.7 constant_dynamic-update-slice_fusion.14
  48.7 0.8 constant_dynamic-update-slice_fusion.13
  49.4 0.7 constant_dynamic-update-slice_fusion.12
  50.2 0.8 constant_dynamic-update-slice_fusion.11
  50.9 0.7 constant_dynamic-update-slice_fusion.10
  51.7 0.7 constant_dynamic-update-slice_fusion.9
  52.4 0.8 constant_dynamic-update-slice_fusion.8
  53.2 0.8 constant_dynamic-update-slice_fusion.7
  53.9 0.8 constant_dynamic-update-slice_fusion.6
  54.7 0.8 constant_dynamic-update-slice_fusion.5
  55.4 0.8 constant_dynamic-update-slice_fusion.4
  56.2 0.8 constant_dynamic-update-slice_fusion.3
  57.0 0.8 constant_dynamic-update-slice_fusion.2
  57.7 0.7 constant_dynamic-update-slice_fusion.1
  58.5 0.7 constant_dynamic-update-slice_fusion
  59.2 38.1 %all-to-all-done = bf16[16,5,32,1024]{3,2,1,0:T(8,128)(2,1)} async-done(((bf16[16,5,32,1024]{3,2,1,0:T(8,128)(2,1)}), bf16[16,5,32,1024]{3,2,1,0:T(8,128)(2,1)}, u32[]{:S(2)}, u32[]{:S(2)}) %all-to-all-start) | async-done | bytes 5242912 | tf_op jit(solution)/shard_map/all_to_all | solution.py:14
  97.3 3.1 %copy.54 = bf16[5,16,32,1024]{3,2,1,0:T(8,128)(2,1)S(1)} copy(bf16[5,16,32,1024]{3,2,0,1:T(8,128)(2,1)} %bitcast) | data formatting | bytes 10485760 | tf_op jit(solution)/shard_map/reshape | solution.py:13
  100.4 5.5 %fusion.11 = (f32[5,256]{1,0:T(8,128)S(1)}, f32[5,512]{1,0:T(8,128)S(1)}, f32[5,256,512]{2,1,0:T(8,128)S(1)}) fusion(pred[5,256]{1,0:T(8,128)(4,1)S(1)} %broadcast_compare_fusion.1, pred[5,512]{1,0:T(8,128)(4,1)S(1)} %broadcast_compare_fusion, bf16[5,512,1024]{2,1,0:T(8,128)(2,1)S(1)} %bitcast.349, ...), kind=kOutput, calls=%fused_computation.30 | convolution fusion | flops 1345450240 | bytes 10504964 | tf_op jit(solution)/shard_map/prd,pcd->prc/dot_general | solution.py:147
  106.0 1.5 copy-done.3
  107.5 1.9 fusion
  109.4 1.9 collective-permute-start.7
  111.4 0.8 collective-permute-done.7
  112.9 2.8 %collective-permute-start.9 = (f32[2,5,256]{2,1,0:T(8,128)S(1)}, f32[2,5,256]{2,1,0:T(8,128)S(1)}, u32[]{:S(2)}, u32[]{:S(2)}) collective-permute-start(f32[2,5,256]{2,1,0:T(8,128)S(1)} %get-tuple-element.34), channel_id=1, source_target_pairs={{0,64},{16,80},{32,96},{48,112},{64,0},{80,16},{96,32},{112,48},{1... | collective-permute-start | bytes 30728 | tf_op jit(solution)/shard_map/ppermute | solution.py:52
  116.0 2.4 collective-permute-start.10
  118.5 1.7 collective-permute-start.15
  120.2 1.0 collective-permute-start.17
  121.9 1.0 collective-permute-done.16
  124.4 2.8 %collective-permute-start.19 = (f32[3,5,512]{2,0,1:T(4,128)S(1)}, f32[3,5,512]{2,0,1:T(4,128)S(1)}, u32[]{:S(2)}, u32[]{:S(2)}) collective-permute-start(f32[3,5,512]{2,0,1:T(4,128)S(1)} %get-tuple-element.30), channel_id=1, source_target_pairs={{0,8},{1,9},{2,10},{3,11},{4,12},{5,13},{6,14},{7,15},{8,0},{9,1},... | collective-permute-start | bytes 92168 | tf_op jit(solution)/shard_map/ppermute | solution.py:52
  127.2 2.7 %collective-permute-start.20 = (f32[3,5,512]{2,0,1:T(4,128)S(1)}, f32[3,5,512]{2,0,1:T(4,128)S(1)}, u32[]{:S(2)}, u32[]{:S(2)}) collective-permute-start(f32[3,5,512]{2,0,1:T(4,128)S(1)} %get-tuple-element.30), channel_id=1, source_target_pairs={{0,12},{1,13},{2,14},{3,15},{4,0},{5,1},{6,2},{7,3},{8,4},{9,5},{1... | collective-permute-start | bytes 92168 | tf_op jit(solution)/shard_map/ppermute | solution.py:52
  130.1 1.2 collective-permute-done.18
  132.3 2.7 %fusion.4 = bf16[5,512,256]{1,2,0:T(8,128)(2,1)S(1)} fusion(f32[5,256,512]{2,1,0:T(8,128)} %copy-done.3, f32[5,256]{1,0:T(8,128)S(1)} %get-tuple-element.9, f32[5,512]{1,0:T(8,128)S(1)} %get-tuple-element.13, f32[5]{0:T(128)S(1)} %get-tuple-element.40, pred[5,256]{1,0:T(8,128)(4,1)S(1)} %broadcast_compare_fusion.1, pred[5,512]{1,0:T(8,128)(4,1)S(1)} %broadcast_compare_fusion), kind=kLoop, calls=%fused_computation.15 | loop fusion | flops 5898240 | bytes 3951380 | tf_op jit(solution)/shard_map/convert_element_type | solution.py:168
  135.1 7.3 %broadcast_multiply_fusion = f32[5,512,1024]{2,1,0:T(8,128)} fusion(bf16[5,512,256]{1,2,0:T(8,128)(2,1)S(1)} %fusion.4, bf16[5,512,1024]{2,1,0:T(8,128)(2,1)} %constant_dynamic-update-slice_fusion, s32[]{:T(128)S(6)} %select_n.293), kind=kOutput, calls=%fused_computation.9 | convolution fusion | flops 1344798720 | bytes 14417924 | tf_op jit(solution)/shard_map/prc,pcd->prd/dot_general | solution.py:171
  142.8 4.0 %broadcast_multiply_fusion.1 = f32[5,256,1024]{2,1,0:T(8,128)S(1)} fusion(bf16[5,512,256]{1,2,0:T(8,128)(2,1)S(1)} %fusion.4, bf16[5,512,1024]{2,1,0:T(8,128)(2,1)} %bitcast.350), kind=kOutput, calls=%fused_computation.21 | convolution fusion | flops 1343488000 | bytes 11796480 | tf_op jit(solution)/shard_map/prc,prd->pcd/dot_general | solution.py:175
  147.0 2.0 maximum_maximum_fusion
  149.1 0.8 copy-done.1
  149.9 4.1 %collective-permute-start.21 = (f32[648,1024]{1,0:T(8,128)}, f32[648,1024]{1,0:T(8,128)}, u32[]{:S(2)}, u32[]{:S(2)}) collective-permute-start(f32[648,1024]{1,0:T(8,128)} %maximum_maximum_fusion), channel_id=1, source_target_pairs={{0,16},{16,0},{32,48},{48,32},{64,80},{80,64},{96,112},{112,96},{1... | collective-permute-start | bytes 7962632 | tf_op jit(solution)/shard_map/ppermute | solution.py:104
  154.0 4.9 %collective-permute-done.21 = f32[648,1024]{1,0:T(8,128)} collective-permute-done((f32[648,1024]{1,0:T(8,128)}, f32[648,1024]{1,0:T(8,128)}, u32[]{:S(2)}, u32[]{:S(2)}) %collective-permute-start.21) | collective-permute-done | bytes 2654240 | tf_op jit(solution)/shard_map/ppermute | solution.py:104
  159.0 2.1 slice.312
  161.1 0.8 bitcast_add_fusion
  162.1 0.8 slice_add_fusion
  163.0 18.0 %collective-permute-done.22 = f32[168,1024]{1,0:T(8,128)S(1)} collective-permute-done((f32[168,1024]{1,0:T(8,128)S(1)}, f32[168,1024]{1,0:T(8,128)S(1)}, u32[]{:S(2)}, u32[]{:S(2)}) %collective-permute-start.22) | collective-permute-done | bytes 688160 | tf_op jit(solution)/shard_map/ppermute | solution.py:117
  181.1 17.0 %collective-permute-done.23 = f32[168,1024]{1,0:T(8,128)S(1)} collective-permute-done((f32[168,1024]{1,0:T(8,128)S(1)}, f32[168,1024]{1,0:T(8,128)S(1)}, u32[]{:S(2)}, u32[]{:S(2)}) %collective-permute-start.23) | collective-permute-done | bytes 688160 | tf_op jit(solution)/shard_map/ppermute | solution.py:117
  198.4 2.8 %collective-permute-done.11 = f32[5]{0:T(128)S(1)} collective-permute-done((f32[5]{0:T(128)S(1)}, f32[5]{0:T(128)S(1)}, u32[]{:S(2)}, u32[]{:S(2)}) %collective-permute-start.11) | collective-permute-done | bytes 52 | tf_op jit(solution)/shard_map/ppermute | solution.py:65
  201.2 0.8 collective-permute-start.12
  202.0 3.1 %collective-permute-done.12 = f32[5]{0:T(128)S(1)} collective-permute-done((f32[5]{0:T(128)S(1)}, f32[5]{0:T(128)S(1)}, u32[]{:S(2)}, u32[]{:S(2)}) %collective-permute-start.12) | collective-permute-done | bytes 52 | tf_op jit(solution)/shard_map/ppermute | solution.py:65
  205.1 2.8 %collective-permute-done.13 = f32[5]{0:T(128)S(1)} collective-permute-done((f32[5]{0:T(128)S(1)}, f32[5]{0:T(128)S(1)}, u32[]{:S(2)}, u32[]{:S(2)}) %collective-permute-start.13) | collective-permute-done | bytes 52 | tf_op jit(solution)/shard_map/ppermute | solution.py:65
  207.9 2.7 %collective-permute-start.14 = (f32[5]{0:T(128)S(1)}, f32[5]{0:T(128)S(1)}, u32[]{:S(2)}, u32[]{:S(2)}) collective-permute-start(f32[5]{0:T(128)S(1)} %fusion.88), channel_id=1, source_target_pairs={{0,8},{1,9},{2,10},{3,11},{4,12},{5,13},{6,14},{7,15},{8,0},{9,1},... | collective-permute-start | bytes 68 | tf_op jit(solution)/shard_map/ppermute | solution.py:65
  210.6 3.8 %collective-permute-done.24 = f32[168,1024]{1,0:T(8,128)S(1)} collective-permute-done((f32[168,1024]{1,0:T(8,128)S(1)}, f32[168,1024]{1,0:T(8,128)S(1)}, u32[]{:S(2)}, u32[]{:S(2)}) %collective-permute-start.24) | collective-permute-done | bytes 688160 | tf_op jit(solution)/shard_map/ppermute | solution.py:117
  216.0 16.8 %reduce-scatter.2.cloned.1.call-done = f32[5,32,1024]{2,1,0:T(8,128)} async-done(((f32[5,512,1024]{2,1,0:T(8,128)}), f32[5,32,1024]{2,1,0:T(8,128)}) %reduce-scatter.2.cloned.1.call-update) | async-done | bytes 655376 | tf_op jit(solution)/shard_map/reduce_scatter | solution.py:178
  232.9 2.4 fusion.16
  (104 shorter events, 8.0 us)
Async XLA Ops:
  11.2 8.9 %copy-start.4 = (bf16[5,32,1024]{2,1,0:T(8,128)(2,1)S(1)}, bf16[5,32,1024]{2,1,0:T(8,128)(2,1)}, u32[]{:S(2)}) copy-start(bf16[5,32,1024]{2,1,0:T(8,128)(2,1)} %param.7) | copy-start | bytes 983044
  11.2 11.2 %copy-start.5 = (bf16[5,32,1024]{2,1,0:T(8,128)(2,1)S(1)}, bf16[5,32,1024]{2,1,0:T(8,128)(2,1)}, u32[]{:S(2)}) copy-start(bf16[5,32,1024]{2,1,0:T(8,128)(2,1)} %param.6) | copy-start | bytes 983044
  11.2 11.4 %copy-start.6 = (s32[5]{0:T(128)S(1)}, s32[5]{0:T(128)}, u32[]{:S(2)}) copy-start(s32[5]{0:T(128)} %param.8) | copy-start | bytes 64
  11.2 11.6 %copy-start.7 = (f32[5]{0:T(128)S(1)}, f32[5]{0:T(128)}, u32[]{:S(2)}) copy-start(f32[5]{0:T(128)} %param.9) | copy-start | bytes 64
  11.2 86.1 %all-to-all-start = ((bf16[16,5,32,1024]{3,2,1,0:T(8,128)(2,1)}), bf16[16,5,32,1024]{3,2,1,0:T(8,128)(2,1)}, u32[]{:S(2)}, u32[]{:S(2)}) async-start(bf16[16,5,32,1024]{3,2,1,0:T(8,128)(2,1)} %stack.92), calls=%async_computation | async-start | bytes 10485760 | tf_op jit(solution)/shard_map/all_to_all | solution.py:14
  20.0 212.9 %reduce-scatter.2.cloned.1.call-start = ((), (), s32[]{:S(2)}) async-start(), calls=%async_computation.2 | async-start | bytes 11141120 | tf_op jit(solution)/shard_map/reduce_scatter | solution.py:178
  20.0 15.2 %collective-permute-start.4 = (bf16[5,32,1024]{2,1,0:T(8,128)(2,1)S(1)}, bf16[5,32,1024]{2,1,0:T(8,128)(2,1)S(1)}, u32[]{:S(2)}, u32[]{:S(2)}) collective-permute-start(bf16[5,32,1024]{2,1,0:T(8,128)(2,1)S(1)} %copy-done.4), channel_id=1, source_target_pairs={{0,112},{16,0},{32,16},{48,32},{64,48},{80,64},{96,80},{112,96},{1... | collective-permute-start | bytes 983048 | tf_op jit(solution)/shard_map/ppermute | solution.py:89
  21.0 5.1 %collective-permute-start = (bf16[5,32,1024]{2,1,0:T(8,128)(2,1)S(1)}, bf16[5,32,1024]{2,1,0:T(8,128)(2,1)S(1)}, u32[]{:S(2)}, u32[]{:S(2)}) collective-permute-start(bf16[5,32,1024]{2,1,0:T(8,128)(2,1)S(1)} %copy-done.4), channel_id=1, source_target_pairs={{0,16},{16,32},{32,48},{48,64},{64,80},{80,96},{96,112},{112,0},{1... | collective-permute-start | bytes 983048 | tf_op jit(solution)/shard_map/ppermute | solution.py:86
  26.1 6.5 %collective-permute-start.1 = (bf16[5,32,1024]{2,1,0:T(8,128)(2,1)S(1)}, bf16[5,32,1024]{2,1,0:T(8,128)(2,1)S(1)}, u32[]{:S(2)}, u32[]{:S(2)}) collective-permute-start(bf16[5,32,1024]{2,1,0:T(8,128)(2,1)S(1)} %collective-permute-done), channel_id=1, source_target_pairs={{0,16},{16,32},{32,48},{48,64},{64,80},{80,96},{96,112},{112,0},{1... | collective-permute-start | bytes 983048 | tf_op jit(solution)/shard_map/ppermute | solution.py:86
  32.6 6.8 %collective-permute-start.2 = (bf16[5,32,1024]{2,1,0:T(8,128)(2,1)S(1)}, bf16[5,32,1024]{2,1,0:T(8,128)(2,1)S(1)}, u32[]{:S(2)}, u32[]{:S(2)}) collective-permute-start(bf16[5,32,1024]{2,1,0:T(8,128)(2,1)S(1)} %collective-permute-done.1), channel_id=1, source_target_pairs={{0,16},{16,32},{32,48},{48,64},{64,80},{80,96},{96,112},{112,0},{1... | collective-permute-start | bytes 983048 | tf_op jit(solution)/shard_map/ppermute | solution.py:86
  35.2 6.9 %collective-permute-start.5 = (bf16[5,32,1024]{2,1,0:T(8,128)(2,1)S(1)}, bf16[5,32,1024]{2,1,0:T(8,128)(2,1)S(1)}, u32[]{:S(2)}, u32[]{:S(2)}) collective-permute-start(bf16[5,32,1024]{2,1,0:T(8,128)(2,1)S(1)} %collective-permute-done.4), channel_id=1, source_target_pairs={{0,112},{16,0},{32,16},{48,32},{64,48},{80,64},{96,80},{112,96},{1... | collective-permute-start | bytes 983048 | tf_op jit(solution)/shard_map/ppermute | solution.py:89
  39.4 7.7 %collective-permute-start.3 = (bf16[5,32,1024]{2,1,0:T(8,128)(2,1)S(1)}, bf16[5,32,1024]{2,1,0:T(8,128)(2,1)S(1)}, u32[]{:S(2)}, u32[]{:S(2)}) collective-permute-start(bf16[5,32,1024]{2,1,0:T(8,128)(2,1)S(1)} %collective-permute-done.2), channel_id=1, source_target_pairs={{0,16},{16,32},{32,48},{48,64},{64,80},{80,96},{96,112},{112,0},{1... | collective-permute-start | bytes 983048 | tf_op jit(solution)/shard_map/ppermute | solution.py:86
  42.1 10.3 %collective-permute-start.6 = (bf16[5,32,1024]{2,1,0:T(8,128)(2,1)S(1)}, bf16[5,32,1024]{2,1,0:T(8,128)(2,1)S(1)}, u32[]{:S(2)}, u32[]{:S(2)}) collective-permute-start(bf16[5,32,1024]{2,1,0:T(8,128)(2,1)S(1)} %collective-permute-done.5), channel_id=1, source_target_pairs={{0,112},{16,0},{32,16},{48,32},{64,48},{80,64},{96,80},{112,96},{1... | collective-permute-start | bytes 983048 | tf_op jit(solution)/shard_map/ppermute | solution.py:89
  100.4 5.6 %copy-start = (bf16[5,16,32,1024]{3,2,1,0:T(8,128)(2,1)}, bf16[5,16,32,1024]{3,2,1,0:T(8,128)(2,1)S(1)}, u32[]{:S(2)}) copy-start(bf16[5,16,32,1024]{3,2,1,0:T(8,128)(2,1)S(1)} %copy.54) | copy-start | bytes 15728644
  106.0 1.5 copy-start.3
  109.4 2.7 %collective-permute-start.7 = (f32[2,5,256]{2,1,0:T(8,128)S(1)}, f32[2,5,256]{2,1,0:T(8,128)S(1)}, u32[]{:S(2)}, u32[]{:S(2)}) collective-permute-start(f32[2,5,256]{2,1,0:T(8,128)S(1)} %get-tuple-element.36), channel_id=1, source_target_pairs={{0,16},{16,0},{32,48},{48,32},{64,80},{80,64},{96,112},{112,96},{1... | collective-permute-start | bytes 30728 | tf_op jit(solution)/shard_map/ppermute | solution.py:52
  112.9 7.4 %collective-permute-start.9 = (f32[2,5,256]{2,1,0:T(8,128)S(1)}, f32[2,5,256]{2,1,0:T(8,128)S(1)}, u32[]{:S(2)}, u32[]{:S(2)}) collective-permute-start(f32[2,5,256]{2,1,0:T(8,128)S(1)} %get-tuple-element.34), channel_id=1, source_target_pairs={{0,64},{16,80},{32,96},{48,112},{64,0},{80,16},{96,32},{112,48},{1... | collective-permute-start | bytes 30728 | tf_op jit(solution)/shard_map/ppermute | solution.py:52
  115.7 5.6 %collective-permute-start.8 = (f32[2,5,256]{2,1,0:T(8,128)S(1)}, f32[2,5,256]{2,1,0:T(8,128)S(1)}, u32[]{:S(2)}, u32[]{:S(2)}) collective-permute-start(f32[2,5,256]{2,1,0:T(8,128)S(1)} %get-tuple-element.34), channel_id=1, source_target_pairs={{0,32},{16,48},{32,64},{48,80},{64,96},{80,112},{96,0},{112,16},{1... | collective-permute-start | bytes 30728 | tf_op jit(solution)/shard_map/ppermute | solution.py:52
  116.0 5.3 %collective-permute-start.10 = (f32[2,5,256]{2,1,0:T(8,128)S(1)}, f32[2,5,256]{2,1,0:T(8,128)S(1)}, u32[]{:S(2)}, u32[]{:S(2)}) collective-permute-start(f32[2,5,256]{2,1,0:T(8,128)S(1)} %get-tuple-element.34), channel_id=1, source_target_pairs={{0,96},{16,112},{32,0},{48,16},{64,32},{80,48},{96,64},{112,80},{1... | collective-permute-start | bytes 30728 | tf_op jit(solution)/shard_map/ppermute | solution.py:52
  118.4 4.5 %collective-permute-start.16 = (f32[3,5,512]{2,0,1:T(4,128)S(1)}, f32[3,5,512]{2,0,1:T(4,128)S(1)}, u32[]{:S(2)}, u32[]{:S(2)}) collective-permute-start(f32[3,5,512]{2,0,1:T(4,128)S(1)} %get-tuple-element.32), channel_id=1, source_target_pairs={{0,2},{1,3},{2,0},{3,1},{4,6},{5,7},{6,4},{7,5},{8,10},{9,11},{10,... | collective-permute-start | bytes 92168 | tf_op jit(solution)/shard_map/ppermute | solution.py:52
  118.5 4.6 %collective-permute-start.15 = (f32[3,5,512]{2,0,1:T(4,128)S(1)}, f32[3,5,512]{2,0,1:T(4,128)S(1)}, u32[]{:S(2)}, u32[]{:S(2)}) collective-permute-start(f32[3,5,512]{2,0,1:T(4,128)S(1)} %get-tuple-element.32), channel_id=1, source_target_pairs={{0,1},{1,2},{2,3},{3,0},{4,5},{5,6},{6,7},{7,4},{8,9},{9,10},{10,1... | collective-permute-start | bytes 92168 | tf_op jit(solution)/shard_map/ppermute | solution.py:52
  120.2 3.1 %collective-permute-start.17 = (f32[3,5,512]{2,0,1:T(4,128)S(1)}, f32[3,5,512]{2,0,1:T(4,128)S(1)}, u32[]{:S(2)}, u32[]{:S(2)}) collective-permute-start(f32[3,5,512]{2,0,1:T(4,128)S(1)} %get-tuple-element.32), channel_id=1, source_target_pairs={{0,3},{1,0},{2,1},{3,2},{4,7},{5,4},{6,5},{7,6},{8,11},{9,8},{10,9... | collective-permute-start | bytes 92168 | tf_op jit(solution)/shard_map/ppermute | solution.py:52
  124.4 5.7 %collective-permute-start.19 = (f32[3,5,512]{2,0,1:T(4,128)S(1)}, f32[3,5,512]{2,0,1:T(4,128)S(1)}, u32[]{:S(2)}, u32[]{:S(2)}) collective-permute-start(f32[3,5,512]{2,0,1:T(4,128)S(1)} %get-tuple-element.30), channel_id=1, source_target_pairs={{0,8},{1,9},{2,10},{3,11},{4,12},{5,13},{6,14},{7,15},{8,0},{9,1},... | collective-permute-start | bytes 92168 | tf_op jit(solution)/shard_map/ppermute | solution.py:52
  127.2 4.1 %collective-permute-start.18 = (f32[3,5,512]{2,0,1:T(4,128)S(1)}, f32[3,5,512]{2,0,1:T(4,128)S(1)}, u32[]{:S(2)}, u32[]{:S(2)}) collective-permute-start(f32[3,5,512]{2,0,1:T(4,128)S(1)} %get-tuple-element.30), channel_id=1, source_target_pairs={{0,4},{1,5},{2,6},{3,7},{4,8},{5,9},{6,10},{7,11},{8,12},{9,13},{1... | collective-permute-start | bytes 92168 | tf_op jit(solution)/shard_map/ppermute | solution.py:52
  127.2 4.1 %collective-permute-start.20 = (f32[3,5,512]{2,0,1:T(4,128)S(1)}, f32[3,5,512]{2,0,1:T(4,128)S(1)}, u32[]{:S(2)}, u32[]{:S(2)}) collective-permute-start(f32[3,5,512]{2,0,1:T(4,128)S(1)} %get-tuple-element.30), channel_id=1, source_target_pairs={{0,12},{1,13},{2,14},{3,15},{4,0},{5,1},{6,2},{7,3},{8,4},{9,5},{1... | collective-permute-start | bytes 92168 | tf_op jit(solution)/shard_map/ppermute | solution.py:52
  146.8 3.1 %copy-start.1 = (f32[5,256,1024]{2,1,0:T(8,128)}, f32[5,256,1024]{2,1,0:T(8,128)S(1)}, u32[]{:S(2)}) copy-start(f32[5,256,1024]{2,1,0:T(8,128)S(1)} %broadcast_multiply_fusion.1) | copy-start | bytes 15728644
  149.9 9.1 %collective-permute-start.21 = (f32[648,1024]{1,0:T(8,128)}, f32[648,1024]{1,0:T(8,128)}, u32[]{:S(2)}, u32[]{:S(2)}) collective-permute-start(f32[648,1024]{1,0:T(8,128)} %maximum_maximum_fusion), channel_id=1, source_target_pairs={{0,16},{16,0},{32,48},{48,32},{64,80},{80,64},{96,112},{112,96},{1... | collective-permute-start | bytes 7962632 | tf_op jit(solution)/shard_map/ppermute | solution.py:104
  154.0 7.0 %copy-start.2 = (f32[5,256,1024]{2,1,0:T(8,128)S(1)}, f32[5,256,1024]{2,1,0:T(8,128)}, u32[]{:S(2)}) copy-start(f32[5,256,1024]{2,1,0:T(8,128)} %copy-done.1) | copy-start | bytes 15728644
  162.9 18.0 %collective-permute-start.22 = (f32[168,1024]{1,0:T(8,128)S(1)}, f32[168,1024]{1,0:T(8,128)S(1)}, u32[]{:S(2)}, u32[]{:S(2)}) collective-permute-start(f32[168,1024]{1,0:T(8,128)S(1)} %pad_maximum_fusion.3), channel_id=1, source_target_pairs={{0,32},{16,48},{32,64},{48,80},{64,96},{80,112},{96,0},{112,16},{1... | collective-permute-start | bytes 2064392 | tf_op jit(solution)/shard_map/ppermute | solution.py:117
  181.0 17.1 %collective-permute-start.23 = (f32[168,1024]{1,0:T(8,128)S(1)}, f32[168,1024]{1,0:T(8,128)S(1)}, u32[]{:S(2)}, u32[]{:S(2)}) collective-permute-start(f32[168,1024]{1,0:T(8,128)S(1)} %fusion.12), channel_id=1, source_target_pairs={{0,32},{16,48},{32,64},{48,80},{64,96},{80,112},{96,0},{112,16},{1... | collective-permute-start | bytes 2064392 | tf_op jit(solution)/shard_map/ppermute | solution.py:117
  198.2 16.2 %collective-permute-start.24 = (f32[168,1024]{1,0:T(8,128)S(1)}, f32[168,1024]{1,0:T(8,128)S(1)}, u32[]{:S(2)}, u32[]{:S(2)}) collective-permute-start(f32[168,1024]{1,0:T(8,128)S(1)} %fusion.13), channel_id=1, source_target_pairs={{0,32},{16,48},{32,64},{48,80},{64,96},{80,112},{96,0},{112,16},{1... | collective-permute-start | bytes 2064392 | tf_op jit(solution)/shard_map/ppermute | solution.py:117
  198.4 2.8 %collective-permute-start.11 = (f32[5]{0:T(128)S(1)}, f32[5]{0:T(128)S(1)}, u32[]{:S(2)}, u32[]{:S(2)}) collective-permute-start(f32[5]{0:T(128)S(1)} %get-tuple-element.8), channel_id=1, source_target_pairs={{0,1},{1,0},{2,3},{3,2},{4,5},{5,4},{6,7},{7,6},{8,9},{9,8},{10,11... | collective-permute-start | bytes 68 | tf_op jit(solution)/shard_map/ppermute | solution.py:65
  201.2 3.9 %collective-permute-start.12 = (f32[5]{0:T(128)S(1)}, f32[5]{0:T(128)S(1)}, u32[]{:S(2)}, u32[]{:S(2)}) collective-permute-start(f32[5]{0:T(128)S(1)} %fusion.90), channel_id=1, source_target_pairs={{0,2},{1,3},{2,0},{3,1},{4,6},{5,7},{6,4},{7,5},{8,10},{9,11},{10,... | collective-permute-start | bytes 68 | tf_op jit(solution)/shard_map/ppermute | solution.py:65
  205.1 2.8 %collective-permute-start.13 = (f32[5]{0:T(128)S(1)}, f32[5]{0:T(128)S(1)}, u32[]{:S(2)}, u32[]{:S(2)}) collective-permute-start(f32[5]{0:T(128)S(1)} %fusion.89), channel_id=1, source_target_pairs={{0,4},{1,5},{2,6},{3,7},{4,0},{5,1},{6,2},{7,3},{8,12},{9,13},{10,... | collective-permute-start | bytes 68 | tf_op jit(solution)/shard_map/ppermute | solution.py:65
  207.9 6.9 %collective-permute-start.14 = (f32[5]{0:T(128)S(1)}, f32[5]{0:T(128)S(1)}, u32[]{:S(2)}, u32[]{:S(2)}) collective-permute-start(f32[5]{0:T(128)S(1)} %fusion.88), channel_id=1, source_target_pairs={{0,8},{1,9},{2,10},{3,11},{4,12},{5,13},{6,14},{7,15},{8,0},{9,1},... | collective-permute-start | bytes 68 | tf_op jit(solution)/shard_map/ppermute | solution.py:65
Sparse Core Ops, SparseCore 0:
  142.5 90.2 reduce-scatter.1
